TPU v7x, 32 devices: a whole 2x2x4 slice. The times are simulated.
32 devices in a mesh: groups: 2 (over y), pairs: 4 (over z), mp: 4 (over x, core).
Axes of the slice: x: 2, y: 2, z: 4, core: 2. Of those that a mesh axis runs over, the one named last changes fastest.
Arguments:
- tokens: bfloat16 [512, 768], P(('groups', 'pairs'), 'mp'), parts along dimension 0, may hold values from -6 to 6
- pair_list: int32 [16, 2], P(('groups', 'pairs')), parts along dimension 0, may hold values from 0 to 7, as said below
- confidence: float32 [16, 64], P(('groups', 'pairs')), parts along dimension 0, may hold values from 0.1 to 10
- gain_self: float32 [768], replicated, may hold values from 0.1 to 1.9
- gain_query: float32 [768], replicated, may hold values from 0.1 to 1.9
- gain_context: float32 [768], replicated, may hold values from 0.1 to 1.9
- gain_mlp: float32 [768], replicated, may hold values from 0.1 to 1.9
- self_qkv: bfloat16 [3, 768, 768], P(None, None, 'mp'), may hold values from -1 to 1
- self_out: bfloat16 [768, 768], P('mp'), may hold values from -0.21875 to 0.21875
- cross_query: bfloat16 [768, 768], P(None, 'mp'), may hold values from -1 to 1
- cross_kv: bfloat16 [2, 768, 768], P(None, None, 'mp'), may hold values from -1 to 1
- cross_out: bfloat16 [768, 768], P('mp'), may hold values from -0.21875 to 0.21875
- mlp_up: bfloat16 [768, 3072], P(None, 'mp'), may hold values from -0.21875 to 0.21875
- mlp_down: bfloat16 [3072, 768], P('mp'), may hold values from -0.109375 to 0.109375
Outputs:
- image_features: bfloat16 [512, 768], P(('groups', 'pairs'), 'mp'), parts along dimension 0
There are 2 independent parts, one for each index of `groups`. A program takes and returns all parts, laid end to end along the dimension named above; an argument that names none is the same for every part. Nothing has to cross between parts.
Inputs may be any that keep to these rules, and one draw needn't show every extreme that they name: `pair_list`: in each block of 2 consecutive pairs the 4 images named are distinct and have distinct owners, the owner of image i being i // 2; the images of each owner are named in exactly 4 blocks; some images are named by no pair.
All inputs are finite; a program needn't handle non-finite values.
Results may differ from a plain program's by a relative error of at most 0.012.
Values may be sent and summed in bfloat16 or wider, within the bound.
No kernel may reach another device: no remote copies, remote signals or barrier semaphores. Data moves between devices by JAX's collectives and lax.ppermute only.
A program may use at most 64 MiB of HBM per device.

v0:
```python
import jax
import jax.numpy as jnp
from jax import lax
from jax.sharding import PartitionSpec as P

HEAD = 64
TOKS = 32
EPSILON = 1e-06


def layer_norm(values, gain):
    center = values - jnp.mean(values, axis=-1, keepdims=True)
    spread = jnp.mean(center * center, axis=-1, keepdims=True)
    return (center * lax.rsqrt(spread + EPSILON) * gain).astype(jnp.bfloat16)


def attend(query, keys, values, views_n):
    rows_n, width = query.shape
    heads_n = width // HEAD
    qh = query.reshape(views_n, TOKS, heads_n, HEAD)
    kh = keys.reshape(views_n, TOKS, heads_n, HEAD)
    vh = values.reshape(views_n, TOKS, heads_n, HEAD)
    scores = jnp.einsum("vqhc,vkhc->vhqk", qh, kh, preferred_element_type=jnp.float32) * HEAD ** (
        -0.5
    )
    probs = jax.nn.softmax(scores, axis=-1).astype(jnp.bfloat16)
    mixed = jnp.einsum("vhqk,vkhc->vqhc", probs, vh, preferred_element_type=jnp.float32)
    return mixed.astype(jnp.bfloat16).reshape(rows_n, width)


def partner(values):
    shape = values.shape
    paired = values.reshape((shape[0] // 2, 2) + shape[1:])
    return jnp.flip(paired, axis=1).reshape(shape)


def summed_full(term):
    return lax.psum(term.astype(jnp.bfloat16), "mp").astype(jnp.float32)


def per_device(
    tokens,
    pair_list,
    confidence,
    gain_self,
    gain_query,
    gain_context,
    gain_mlp,
    self_qkv,
    self_out,
    cross_query,
    cross_kv,
    cross_out,
    mlp_up,
    mlp_down,
):
    quarter = tokens.shape[1]
    img_dev = tokens.shape[0] // TOKS
    pair_dev = pair_list.shape[0]
    views_n = 2 * pair_dev
    owners_n = lax.axis_size("pairs")
    own = lax.axis_index("pairs")
    table = lax.all_gather(pair_list, "pairs", axis=0, tiled=True).reshape(owners_n, views_n)
    wanted = jnp.where(table // img_dev == own, table % img_dev, -1)
    chosen = jnp.max(wanted, axis=1)
    images = tokens.reshape(img_dev, TOKS, quarter)
    picked = jnp.take(images, jnp.maximum(chosen, 0), axis=0)
    outgoing = jnp.where((chosen >= 0)[:, None, None], picked, jnp.zeros_like(picked))
    arrived = lax.all_to_all(outgoing, "pairs", split_axis=0, concat_axis=0, tiled=True)
    source = pair_list.reshape(views_n) // img_dev
    slices = jnp.take(arrived, source, axis=0)
    start = lax.all_gather(slices, "mp", axis=2, tiled=True)
    width = start.shape[2]
    rows_n = views_n * TOKS
    begin = start.astype(jnp.float32).reshape(rows_n, width)
    context = layer_norm(partner(start.astype(jnp.float32)), gain_context).reshape(rows_n, width)
    offset = lax.axis_index("mp") * quarter
    normed = layer_norm(begin, gain_self)
    qkv = jnp.einsum("rd,kdc->krc", normed, self_qkv, preferred_element_type=jnp.float32).astype(
        jnp.bfloat16
    )
    term = jnp.dot(
        attend(qkv[0], qkv[1], qkv[2], views_n), self_out, preferred_element_type=jnp.float32
    )
    resid = begin + summed_full(term)
    normed = layer_norm(resid, gain_query)
    query = jnp.dot(normed, cross_query, preferred_element_type=jnp.float32).astype(jnp.bfloat16)
    keyval = jnp.einsum(
        "rd,kdc->krc", context, cross_kv, preferred_element_type=jnp.float32
    ).astype(jnp.bfloat16)
    term = jnp.dot(
        attend(query, keyval[0], keyval[1], views_n), cross_out, preferred_element_type=jnp.float32
    )
    resid = resid + summed_full(term)
    normed = layer_norm(resid, gain_mlp)
    hidden = jax.nn.gelu(
        jnp.dot(normed, mlp_up, preferred_element_type=jnp.float32), approximate=False
    )
    term = jnp.dot(hidden.astype(jnp.bfloat16), mlp_down, preferred_element_type=jnp.float32)
    resid = resid + summed_full(term)
    final = lax.dynamic_slice_in_dim(resid, offset, quarter, 1)
    conf = confidence.reshape(views_n, TOKS)
    weighted = (final.reshape(views_n, TOKS, quarter) * conf[:, :, None]).reshape(
        views_n, TOKS * quarter
    )
    route = (source[None, :] == jnp.arange(owners_n)[:, None]).astype(jnp.float32)
    back = jnp.dot(route, weighted, precision=lax.Precision.HIGHEST).astype(jnp.bfloat16)
    back_weight = jnp.dot(route, conf, precision=lax.Precision.HIGHEST).astype(jnp.bfloat16)
    got_feat, got_weight = (
        lax.all_to_all(
            back.reshape(owners_n, TOKS, quarter), "pairs", split_axis=0, concat_axis=0, tiled=True
        ),
        lax.all_to_all(back_weight, "pairs", split_axis=0, concat_axis=0, tiled=True),
    )
    owner_match = chosen[None, :] == jnp.arange(img_dev)[:, None]
    numer = jnp.einsum(
        "ij,jtc->itc",
        owner_match.astype(jnp.bfloat16),
        got_feat,
        preferred_element_type=jnp.float32,
    )
    denom = jnp.dot(
        owner_match.astype(jnp.float32),
        got_weight.astype(jnp.float32),
        precision=lax.Precision.HIGHEST,
    )
    result = numer / jnp.maximum(denom, 1.0)[:, :, None]
    return result.astype(jnp.bfloat16).reshape(img_dev * TOKS, quarter)


def solution(mesh):
    return jax.shard_map(
        per_device,
        mesh=mesh,
        in_specs=(
            P(("groups", "pairs"), "mp"),
            P(("groups", "pairs"), None),
            P(("groups", "pairs"), None),
            P(),
            P(),
            P(),
            P(),
            P(None, None, "mp"),
            P("mp", None),
            P(None, "mp"),
            P(None, None, "mp"),
            P("mp", None),
            P(None, "mp"),
            P("mp", None),
        ),
        out_specs=P(("groups", "pairs"), "mp"),
        check_vma=False,
    )
```

profile of v0, /device:TPU:0, one launch (start us, length us, event | category | flops | bytes accessed | tf_op | source)
XLA Modules:
  0.0 180.7 jit_solution(869110114710449456)
XLA Ops:
  6.5 13.0 %all-gather = s32[4,2,2]{2,1,0:T(2,128)S(1)} all-gather(s32[1,2,2]{2,1,0:T(2,128)} %bitcast.90), channel_id=1, replica_groups=mesh['groups'=2,'pairs'=4,'mp'=4] {'pairs'}, dimensions={0}, use_global_device_ids=true | all-gather | bytes 80 | tf_op jit(solution)/shard_map/all_gather | solution.py:63
  20.4 1.3 gather_fusion
  22.4 3.3 %all-to-all-start = ((bf16[4,32,192]{2,1,0:T(8,128)(2,1)}), bf16[4,32,192]{2,1,0:T(8,128)(2,1)S(1)}, u32[]{:S(2)}, u32[]{:S(2)}) async-start(bf16[4,32,192]{2,1,0:T(8,128)(2,1)} %select_select_fusion), calls=%async_computation | async-start | bytes 131072 | tf_op jit(solution)/shard_map/all_to_all | solution.py:69
  27.8 3.6 %all-to-all-done = bf16[4,32,192]{2,1,0:T(8,128)(2,1)S(1)} async-done(((bf16[4,32,192]{2,1,0:T(8,128)(2,1)}), bf16[4,32,192]{2,1,0:T(8,128)(2,1)S(1)}, u32[]{:S(2)}, u32[]{:S(2)}) %all-to-all-start) | async-done | bytes 49184 | tf_op jit(solution)/shard_map/all_to_all | solution.py:69
  32.2 8.6 %all_gather.7 = bf16[4,32,768]{1,0,2:T(4,128)(2,1)S(1)} all-gather(bf16[4,32,192]{1,0,2:T(4,128)(2,1)S(1)} %copy.73), channel_id=1, replica_groups=mesh['groups'=2,'pairs'=4,'mp'=4] {'mp'}, dimensions={2}, use_global_device_ids=true | all-gather | bytes 245760 | tf_op jit(solution)/shard_map/all_gather | solution.py:72
  42.1 0.8 multiply_reduce_fusion.1
  43.6 1.3 convert_element_type.84
  44.9 7.5 %rev.4 = f32[2,2,32,768]{2,1,0,3:T(2,128)S(1)} reverse(f32[2,2,32,768]{2,1,0,3:T(2,128)} %bitcast.83), dimensions={1} | reverse | bytes 786432 | tf_op jit(solution)/shard_map/jit(_flip)/rev | solution.py:34
  52.4 0.8 reduce_sum.93
  53.2 1.1 multiply_reduce_fusion
  56.0 1.6 fusion.122
  58.9 0.9 convolution_convert_fusion.3
  60.7 28.6 %all-reduce.4.cloned.1.call-done = bf16[128,768]{1,0:T(8,128)(2,1)} async-done(((bf16[128,768]{1,0:T(8,128)(2,1)}), bf16[128,768]{1,0:T(8,128)(2,1)}) %all-reduce.4.cloned.1.call-update) | async-done | bytes 196624 | tf_op jit(solution)/shard_map/psum | solution.py:38
  89.3 1.0 fusion.77
  90.4 1.1 multiply_reduce_fusion.3
  92.8 0.9 convolution_convert_fusion.2
  93.9 31.7 %all-reduce.6.cloned.1.call-done = bf16[128,768]{1,0:T(8,128)(2,1)} async-done(((bf16[128,768]{1,0:T(8,128)(2,1)}), bf16[128,768]{1,0:T(8,128)(2,1)}) %all-reduce.6.cloned.1.call-update) | async-done | bytes 196624 | tf_op jit(solution)/shard_map/psum | solution.py:38
  125.6 1.1 fusion.117
  126.9 2.1 %convolution_convert_fusion.1 = bf16[128,768]{1,0:T(8,128)(2,1)} fusion(bf16[768,768]{1,0:T(8,128)(2,1)S(1)} %copy-done, bf16[768,768]{1,0:T(8,128)(2,1)S(1)} %copy-done.13, f32[128,768]{1,0:T(8,128)S(1)} %get-tuple-element.6, f32[768]{0:T(1024)S(1)} %copy-done.14, f32[128]{0:T(128)S(1)} %add_rsqrt_fusion.2, f32[128]{0:T(128)S(1)} %broadcast_multiply_fusion.2), kind=kOutput, calls=%fused_computation.9 | convolution fusion | flops 308871168 | bytes 2953216 | tf_op jit(solution)/shard_map/dot_general | solution.py:99
  129.8 4.6 %all-to-all-start.2 = ((bf16[4,1,32]{2,1,0:T(2,128)(2,1)}), bf16[4,1,32]{2,1,0:T(2,128)(2,1)S(1)}, u32[]{:S(2)}, u32[]{:S(2)}) async-start(bf16[4,1,32]{2,1,0:T(2,128)(2,1)} %copy.94), calls=%async_computation.2 | async-start | bytes 4096 | tf_op jit(solution)/shard_map/all_to_all | solution.py:113
  134.6 26.3 %all-reduce.8.cloned.1.call-done = bf16[128,768]{1,0:T(8,128)(2,1)} async-done(((bf16[128,768]{1,0:T(8,128)(2,1)}), bf16[128,768]{1,0:T(8,128)(2,1)}) %all-reduce.8.cloned.1.call-update) | async-done | bytes 196624 | tf_op jit(solution)/shard_map/psum | solution.py:38
  160.9 1.0 dynamic-slice_add_fusion
  163.0 4.6 %all-to-all-start.1 = ((bf16[4,32,192]{2,1,0:T(8,128)(2,1)}), bf16[4,32,192]{2,1,0:T(8,128)(2,1)S(1)}, u32[]{:S(2)}, u32[]{:S(2)}) async-start(bf16[4,32,192]{2,1,0:T(8,128)(2,1)} %reshape.285), calls=%async_computation.1 | async-start | bytes 131072 | tf_op jit(solution)/shard_map/all_to_all | solution.py:110
  167.8 5.5 %all-to-all-done.1 = bf16[4,32,192]{2,1,0:T(8,128)(2,1)S(1)} async-done(((bf16[4,32,192]{2,1,0:T(8,128)(2,1)}), bf16[4,32,192]{2,1,0:T(8,128)(2,1)S(1)}, u32[]{:S(2)}, u32[]{:S(2)}) %all-to-all-start.1) | async-done | bytes 49184 | tf_op jit(solution)/shard_map/all_to_all | solution.py:110
  (105 shorter events, 14.7 us)
Async XLA Ops:
  6.5 120.3 %copy-start = (bf16[768,768]{1,0:T(8,128)(2,1)S(1)}, bf16[768,768]{1,0:T(8,128)(2,1)}, u32[]{:S(2)}) copy-start(bf16[768,768]{1,0:T(8,128)(2,1)} %param.27) | copy-start | bytes 3538948
  19.8 0.5 copy-start.11
  22.4 9.0 %all-to-all-start = ((bf16[4,32,192]{2,1,0:T(8,128)(2,1)}), bf16[4,32,192]{2,1,0:T(8,128)(2,1)S(1)}, u32[]{:S(2)}, u32[]{:S(2)}) async-start(bf16[4,32,192]{2,1,0:T(8,128)(2,1)} %select_select_fusion), calls=%async_computation | async-start | bytes 131072 | tf_op jit(solution)/shard_map/all_to_all | solution.py:69
  25.7 63.6 %all-reduce.4.cloned.1.call-start = ((), (), s32[]{:S(2)}) async-start(), calls=%async_computation.3 | async-start | bytes 393216 | tf_op jit(solution)/shard_map/psum | solution.py:38
  53.2 1.9 %copy-start.6 = (f32[768]{0:T(1024)S(1)}, f32[768]{0:T(1024)}, u32[]{:S(2)}) copy-start(f32[768]{0:T(1024)} %param.17) | copy-start | bytes 9220
  57.6 1.3 copy-start.3
  57.9 2.0 %copy-start.7 = (f32[768]{0:T(1024)S(1)}, f32[768]{0:T(1024)}, u32[]{:S(2)}) copy-start(f32[768]{0:T(1024)} %param.19) | copy-start | bytes 9220
  58.2 1.9 %copy-start.2 = (bf16[2,768,192]{1,2,0:T(8,128)(2,1)S(1)}, bf16[2,768,192]{1,2,0:T(8,128)(2,1)}, u32[]{:S(2)}) copy-start(bf16[2,768,192]{1,2,0:T(8,128)(2,1)} %param.24) | copy-start | bytes 1769476
  59.8 65.8 %all-reduce.6.cloned.1.call-start = ((), (), s32[]{:S(2)}) async-start(), calls=%async_computation.4 | async-start | bytes 393216 | tf_op jit(solution)/shard_map/psum | solution.py:38
  60.1 31.4 %copy-start.4 = (bf16[768,192]{0,1:T(8,128)(2,1)S(1)}, bf16[768,192]{0,1:T(8,128)(2,1)}, u32[]{:S(2)}) copy-start(bf16[768,192]{0,1:T(8,128)(2,1)} %param.23) | copy-start | bytes 884740
  60.1 31.4 %copy-start.8 = (f32[768]{0:T(1024)S(1)}, f32[768]{0:T(1024)}, u32[]{:S(2)}) copy-start(f32[768]{0:T(1024)} %param.18) | copy-start | bytes 9220
  91.5 1.3 copy-start.5
  92.0 1.8 copy-start.9
  92.0 33.6 %copy-start.1 = (bf16[128,768]{1,0:T(8,128)(2,1)S(1)}, bf16[128,768]{1,0:T(8,128)(2,1)}, u32[]{:S(2)}) copy-start(bf16[128,768]{1,0:T(8,128)(2,1)} %all-reduce.4.cloned.1.call-done) | copy-start | bytes 589828
  92.6 34.3 %copy-start.14 = (f32[768]{0:T(1024)S(1)}, f32[768]{0:T(1024)}, u32[]{:S(2)}) copy-start(f32[768]{0:T(1024)} %param.20) | copy-start | bytes 9220
  93.7 67.2 %all-reduce.8.cloned.1.call-start = ((), (), s32[]{:S(2)}) async-start(), calls=%async_computation.5 | async-start | bytes 393216 | tf_op jit(solution)/shard_map/psum | solution.py:38
  93.9 33.0 %copy-start.13 = (bf16[768,768]{1,0:T(8,128)(2,1)S(1)}, bf16[768,768]{1,0:T(8,128)(2,1)}, u32[]{:S(2)}) copy-start(bf16[768,768]{1,0:T(8,128)(2,1)} %param.26) | copy-start | bytes 3538948
  126.9 2.2 %copy-start.10 = (s32[4]{0:T(128)S(1)}, s32[4]{0:T(128)}, u32[]{:S(2)}) copy-start(s32[4]{0:T(128)} %get-tuple-element.8) | copy-start | bytes 52
  129.1 38.6 %copy-start.12 = (s32[4]{0:T(128)S(1)}, s32[4]{0:T(128)}, u32[]{:S(2)}) copy-start(s32[4]{0:T(128)} %copy-done.11) | copy-start | bytes 52
  129.8 33.2 %all-to-all-start.2 = ((bf16[4,1,32]{2,1,0:T(2,128)(2,1)}), bf16[4,1,32]{2,1,0:T(2,128)(2,1)S(1)}, u32[]{:S(2)}, u32[]{:S(2)}) async-start(bf16[4,1,32]{2,1,0:T(2,128)(2,1)} %copy.94), calls=%async_computation.2 | async-start | bytes 4096 | tf_op jit(solution)/shard_map/all_to_all | solution.py:113
  163.0 10.3 %all-to-all-start.1 = ((bf16[4,32,192]{2,1,0:T(8,128)(2,1)}), bf16[4,32,192]{2,1,0:T(8,128)(2,1)S(1)}, u32[]{:S(2)}, u32[]{:S(2)}) async-start(bf16[4,32,192]{2,1,0:T(8,128)(2,1)} %reshape.285), calls=%async_computation.1 | async-start | bytes 131072 | tf_op jit(solution)/shard_map/all_to_all | solution.py:110
Sparse Core Ops, SparseCore 0:
  59.9 29.3 all-reduce.3
  93.8 31.7 all-reduce.5
  129.2 31.6 all-reduce.7
where the time goes:
time: 181 us
  waiting for transfers between devices  95.8 us (53%)
  blocking collectives  21.6 us (12%)
  local copies, waits for them, and re-layouts  17.5 us (10%)
  between operations  13.6 us (8%)
  starting transfers between devices  12.6 us (7%)
  other arithmetic  12 us (7%)
  matrix products  7.72 us (4%)
    psum x3, waiting for transfers between devices, summed_full(): return lax.psum(term.astype(jnp.bfloat16), 'mp').astype(jnp.float32)  86.6 us
    all_gather x1, blocking collectives, per_device(): lax.all_gather(pair_list, 'pairs', axis=0, tiled=True)  13 us
    all_gather x1, blocking collectives, per_device(): start = lax.all_gather(slices, 'mp', axis=2, tiled=True)  8.6 us
    rev x2, local copies, waits for them, and re-layouts, partner(): return jnp.flip(paired, axis=1).reshape(shape)  8.14 us
    all_to_all x1, waiting for transfers between devices, per_device(): lax.all_to_all(back.reshape(owners_n, TOKS, quarter), 'pairs', split_axis...  5.53 us
    all_to_all x1, starting transfers between devices, per_device(): lax.all_to_all(back_weight, 'pairs', split_axis=0, concat_axis=0, tiled=T...  4.6 us
    all_to_all x1, starting transfers between devices, per_device(): lax.all_to_all(back.reshape(owners_n, TOKS, quarter), 'pairs', split_axis...  4.6 us
    reduce_sum x4, other arithmetic, layer_norm(): center = values - jnp.mean(values, axis=-1, keepdims=True)  3.78 us
  transfers between devices with their start and end apart: 6, of which 5 were waited for; matrix products, arithmetic and copies ran while one was open for 3% of the time, Pallas kernels for 0%

commit v1 on v0

--- a/solution.py
+++ b/solution.py
@@ -35,7 +35,7 @@
 
 
 def summed_full(term):
-    return lax.psum(term.astype(jnp.bfloat16), "mp").astype(jnp.float32)
+    return jnp.sum(lax.all_gather(term.astype(jnp.bfloat16), "mp"), axis=0).astype(jnp.float32)
 
 
 def per_device(

time: 181 us -> 87.4 us (0.48)
  waiting for transfers between devices: 95.8 us -> 8 us
  blocking collectives: 21.6 us -> 47.7 us
  between operations: 13.6 us -> 0.48 us
  other arithmetic: 12 us -> 3.46 us
  local copies, waits for them, and re-layouts: 17.5 us -> 9.82 us
  matrix products: 7.72 us -> 5.69 us
    psum x3 -> x0, waiting for transfers between devices: 86.6 us -> none  [summed_full(): return lax.psum(term.astype(jnp.bfloat16), 'mp').astype(jnp.float32)]
    all_gather x0 -> x3, blocking collectives: none -> 26.2 us  [summed_full(): lax.all_gather(term.astype(jnp.bfloat16), 'mp')]
    rev x2 -> x1, local copies, waits for them, and re-layouts: 8.14 us -> 0.03 us  [partner(): return jnp.flip(paired, axis=1).reshape(shape)]
    reduce_sum x4, other arithmetic: 3.78 us -> 0.48 us  [layer_norm(): center = values - jnp.mean(values, axis=-1, keepdims=True)]
    reduce_sum x4, other arithmetic: 3.23 us -> 0.77 us  [layer_norm(): spread = jnp.mean(center * center, axis=-1, keepdims=True)]
  transfers between devices with their start and end apart: 6 -> 3, of which waited for: 5 -> 2; matrix products, arithmetic and copies ran while one was open for 3% -> 18% of each run, Pallas kernels for 0% -> 0%
where the time goes in v1:
time: 87.4 us; the launch traced here: 86.8 us
  blocking collectives  47.7 us (55%)
  starting transfers between devices  11.6 us (13%)
  local copies, waits for them, and re-layouts  9.82 us (11%)
  waiting for transfers between devices  8 us (9%)
  matrix products  5.69 us (7%)
  other arithmetic  3.46 us (4%)
    all_gather x3, blocking collectives, summed_full(): lax.all_gather(term.astype(jnp.bfloat16), 'mp')  26.2 us
    all_gather x1, blocking collectives, per_device(): lax.all_gather(pair_list, 'pairs', axis=0, tiled=True)  13 us
    all_gather x1, blocking collectives, per_device(): start = lax.all_gather(slices, 'mp', axis=2, tiled=True)  8.6 us
    all_to_all x1, waiting for transfers between devices, per_device(): lax.all_to_all(back.reshape(owners_n, TOKS, quarter), 'pairs', split_axis...  5.53 us
    all_to_all x1, starting transfers between devices, per_device(): lax.all_to_all(back.reshape(owners_n, TOKS, quarter), 'pairs', split_axis...  5.05 us
    all_to_all x1, starting transfers between devices, per_device(): lax.all_to_all(outgoing, 'pairs', split_axis=0, concat_axis=0, tiled=True)  3.28 us
    all_to_all x1, starting transfers between devices, per_device(): lax.all_to_all(back_weight, 'pairs', split_axis=0, concat_axis=0, tiled=T...  3.22 us
    dot_general x1, matrix products, per_device(): jnp.dot(hidden.astype(jnp.bfloat16), mlp_down, preferred_element_type=jnp...  2.72 us
  transfers between devices with their start and end apart: 3, of which 2 were waited for; matrix products, arithmetic and copies ran while one was open for 18% of the time, Pallas kernels for 0%

profile of v1, /device:TPU:0, one launch (start us, length us, event | category | flops | bytes accessed | tf_op | source)
XLA Modules:
  0.0 86.8 jit_solution(9064554680219542718)
XLA Ops:
  0.0 13.0 %all-gather.3 = s32[4,2,2]{2,1,0:T(2,128)S(1)} all-gather(s32[1,2,2]{2,1,0:T(2,128)} %bitcast.102), channel_id=1, replica_groups=mesh['groups'=2,'pairs'=4,'mp'=4] {'pairs'}, dimensions={0}, use_global_device_ids=true | all-gather | bytes 80 | tf_op jit(solution)/shard_map/all_gather | solution.py:63
  13.3 1.3 %gather_fusion = bf16[4,32,192]{2,1,0:T(8,128)(2,1)S(1)} fusion(bf16[2,32,192]{2,1,0:T(8,128)(2,1)} %bitcast.100, s32[1024]{0:T(1024)S(1)} %pad_clamp_fusion.1), kind=kCustom, calls=%fused_computation | custom fusion | bytes 98320 | tf_op jit(solution)/shard_map/jit(_take)/gather | solution.py:67
  14.6 0.7 select_select_fusion
  15.3 3.3 %all-to-all-start = ((bf16[4,32,192]{2,1,0:T(8,128)(2,1)}), bf16[4,32,192]{2,1,0:T(8,128)(2,1)S(1)}, u32[]{:S(2)}, u32[]{:S(2)}) async-start(bf16[4,32,192]{2,1,0:T(8,128)(2,1)} %select_select_fusion), calls=%async_computation | async-start | bytes 131072 | tf_op jit(solution)/shard_map/all_to_all | solution.py:69
  18.6 0.8 reshape.327
  19.4 0.8 reshape.325
  20.2 0.8 mul.147
  21.3 0.6 copy.92
  21.9 2.5 %all-to-all-done = bf16[4,32,192]{2,1,0:T(8,128)(2,1)S(1)} async-done(((bf16[4,32,192]{2,1,0:T(8,128)(2,1)}), bf16[4,32,192]{2,1,0:T(8,128)(2,1)S(1)}, u32[]{:S(2)}, u32[]{:S(2)}) %all-to-all-start) | async-done | bytes 49184 | tf_op jit(solution)/shard_map/all_to_all | solution.py:69
  24.3 3.2 %all-to-all-start.2 = ((bf16[4,1,32]{2,1,0:T(2,128)(2,1)}), bf16[4,1,32]{2,1,0:T(2,128)(2,1)S(1)}, u32[]{:S(2)}, u32[]{:S(2)}) async-start(bf16[4,1,32]{2,1,0:T(2,128)(2,1)} %copy.92), calls=%async_computation.2 | async-start | bytes 4096 | tf_op jit(solution)/shard_map/all_to_all | solution.py:113
  27.6 0.6 gather_fusion.1
  28.4 8.6 %all_gather.25 = bf16[4,32,768]{1,0,2:T(4,128)(2,1)S(1)} all-gather(bf16[4,32,192]{1,0,2:T(4,128)(2,1)S(1)} %copy.73), channel_id=1, replica_groups=mesh['groups'=2,'pairs'=4,'mp'=4] {'mp'}, dimensions={2}, use_global_device_ids=true | all-gather | bytes 245760 | tf_op jit(solution)/shard_map/all_gather | solution.py:72
  37.0 0.5 copy.74
  38.7 0.4 fusion.123
  40.6 8.7 %all-gather = bf16[512,768]{1,0:T(8,128)(2,1)S(1)} all-gather(bf16[128,768]{1,0:T(8,128)(2,1)S(1)} %convolution_convert_fusion.3), channel_id=2, replica_groups=mesh['groups'=2,'pairs'=4,'mp'=4] {'mp'}, dimensions={0}, use_global_device_ids=true | all-gather | bytes 983040 | tf_op jit(solution)/shard_map/all_gather | solution.py:38
  50.1 0.3 copy-done.4
  51.1 0.3 fusion.124
  52.8 8.7 %all-gather.1 = bf16[512,768]{1,0:T(8,128)(2,1)S(1)} all-gather(bf16[128,768]{1,0:T(8,128)(2,1)S(1)} %convolution_convert_fusion.2), channel_id=3, replica_groups=mesh['groups'=2,'pairs'=4,'mp'=4] {'mp'}, dimensions={0}, use_global_device_ids=true | all-gather | bytes 983040 | tf_op jit(solution)/shard_map/all_gather | solution.py:38
  62.4 2.7 %convolution_convert_fusion.1 = bf16[128,768]{1,0:T(8,128)(2,1)S(1)} fusion(bf16[768,768]{1,0:T(8,128)(2,1)S(1)} %copy-done, bf16[768,768]{1,0:T(8,128)(2,1)} %param.26, f32[128,768]{1,0:T(8,128)S(1)} %fusion.28, f32[768]{0:T(1024)S(1)} %copy-done.9, f32[128]{0:T(128)S(1)} %rsqrt.51, f32[128]{0:T(128)S(1)} %div.105), kind=kOutput, calls=%fused_computation.7 | convolution fusion | flops 308871168 | bytes 2953216 | tf_op jit(solution)/shard_map/dot_general | solution.py:99
  65.1 8.7 %all-gather.2 = bf16[512,768]{1,0:T(8,128)(2,1)S(1)} all-gather(bf16[128,768]{1,0:T(8,128)(2,1)S(1)} %convolution_convert_fusion.1), channel_id=4, replica_groups=mesh['groups'=2,'pairs'=4,'mp'=4] {'mp'}, dimensions={0}, use_global_device_ids=true | all-gather | bytes 983040 | tf_op jit(solution)/shard_map/all_gather | solution.py:38
  74.4 0.7 reshape.335
  75.2 5.1 %all-to-all-start.1 = ((bf16[4,32,192]{2,1,0:T(8,128)(2,1)}), bf16[4,32,192]{2,1,0:T(8,128)(2,1)S(1)}, u32[]{:S(2)}, u32[]{:S(2)}) async-start(bf16[4,32,192]{2,1,0:T(8,128)(2,1)} %reshape.335), calls=%async_computation.1 | async-start | bytes 131072 | tf_op jit(solution)/shard_map/all_to_all | solution.py:110
  80.4 5.5 %all-to-all-done.1 = bf16[4,32,192]{2,1,0:T(8,128)(2,1)S(1)} async-done(((bf16[4,32,192]{2,1,0:T(8,128)(2,1)}), bf16[4,32,192]{2,1,0:T(8,128)(2,1)S(1)}, u32[]{:S(2)}, u32[]{:S(2)}) %all-to-all-start.1) | async-done | bytes 49184 | tf_op jit(solution)/shard_map/all_to_all | solution.py:110
  86.1 0.6 copy.94
  (97 shorter events, 8.0 us)
Async XLA Ops:
  0.0 62.2 %copy-start = (bf16[768,768]{1,0:T(8,128)(2,1)S(1)}, bf16[768,768]{1,0:T(8,128)(2,1)}, u32[]{:S(2)}) copy-start(bf16[768,768]{1,0:T(8,128)(2,1)} %param.27) | copy-start | bytes 3538948
  15.3 9.0 %all-to-all-start = ((bf16[4,32,192]{2,1,0:T(8,128)(2,1)}), bf16[4,32,192]{2,1,0:T(8,128)(2,1)S(1)}, u32[]{:S(2)}, u32[]{:S(2)}) async-start(bf16[4,32,192]{2,1,0:T(8,128)(2,1)} %select_select_fusion), calls=%async_computation | async-start | bytes 131072 | tf_op jit(solution)/shard_map/all_to_all | solution.py:69
  24.3 50.8 %all-to-all-start.2 = ((bf16[4,1,32]{2,1,0:T(2,128)(2,1)}), bf16[4,1,32]{2,1,0:T(2,128)(2,1)S(1)}, u32[]{:S(2)}, u32[]{:S(2)}) async-start(bf16[4,1,32]{2,1,0:T(2,128)(2,1)} %copy.92), calls=%async_computation.2 | async-start | bytes 4096 | tf_op jit(solution)/shard_map/all_to_all | solution.py:113
  37.0 1.4 %copy-start.6 = (f32[768]{0:T(1024)S(1)}, f32[768]{0:T(1024)}, u32[]{:S(2)}) copy-start(f32[768]{0:T(1024)} %param.17) | copy-start | bytes 9220
  37.5 1.2 %copy-start.1 = (bf16[3,768,192]{1,2,0:T(8,128)(2,1)S(1)}, bf16[3,768,192]{1,2,0:T(8,128)(2,1)}, u32[]{:S(2)}) copy-start(bf16[3,768,192]{1,2,0:T(8,128)(2,1)} %param.21) | copy-start | bytes 2654212
  39.4 1.0 %copy-start.3 = (bf16[192,768]{1,0:T(8,128)(2,1)S(1)}, bf16[192,768]{1,0:T(8,128)(2,1)}, u32[]{:S(2)}) copy-start(bf16[192,768]{1,0:T(8,128)(2,1)} %param.22) | copy-start | bytes 884740
  49.3 0.7 copy-start.7
  49.4 1.0 %copy-start.4 = (bf16[768,192]{0,1:T(8,128)(2,1)S(1)}, bf16[768,192]{0,1:T(8,128)(2,1)}, u32[]{:S(2)}) copy-start(bf16[768,192]{0,1:T(8,128)(2,1)} %param.23) | copy-start | bytes 884740
  49.7 1.2 %copy-start.8 = (f32[768]{0:T(1024)S(1)}, f32[768]{0:T(1024)}, u32[]{:S(2)}) copy-start(f32[768]{0:T(1024)} %param.19) | copy-start | bytes 9220
  50.0 1.1 %copy-start.2 = (bf16[2,768,192]{1,2,0:T(8,128)(2,1)S(1)}, bf16[2,768,192]{1,2,0:T(8,128)(2,1)}, u32[]{:S(2)}) copy-start(bf16[2,768,192]{1,2,0:T(8,128)(2,1)} %param.24) | copy-start | bytes 1769476
  51.6 1.0 %copy-start.5 = (bf16[192,768]{1,0:T(8,128)(2,1)S(1)}, bf16[192,768]{1,0:T(8,128)(2,1)}, u32[]{:S(2)}) copy-start(bf16[192,768]{1,0:T(8,128)(2,1)} %param.25) | copy-start | bytes 884740
  61.7 0.7 copy-start.9
  75.2 10.8 %all-to-all-start.1 = ((bf16[4,32,192]{2,1,0:T(8,128)(2,1)}), bf16[4,32,192]{2,1,0:T(8,128)(2,1)S(1)}, u32[]{:S(2)}, u32[]{:S(2)}) async-start(bf16[4,32,192]{2,1,0:T(8,128)(2,1)} %reshape.335), calls=%async_computation.1 | async-start | bytes 131072 | tf_op jit(solution)/shard_map/all_to_all | solution.py:110
